TPU v7x, 512 devices: a whole 4x4x16 slice. The times are simulated.
512 devices in a mesh: row: 16 (over z), col: 32 (over y, x, core).
Axes of the slice: x: 4, y: 4, z: 16, core: 2. Of those that a mesh axis runs over, the one named last changes fastest.
Arguments:
- inputs: bfloat16 [2048, 8192], P('col', 'row'), may hold values from -6 to 6
- gate_pre: bfloat16 [2048, 14784], P('row', 'col'), may hold values from -6 to 6
- up_pre: bfloat16 [2048, 14784], P('row', 'col'), may hold values from -6 to 6
- w_gate: bfloat16 [8192, 14784], P('row', 'col'), may hold values from -0.0625 to 0.0625
- w_up: bfloat16 [8192, 14784], P('row', 'col'), may hold values from -0.0625 to 0.0625
- w_down: bfloat16 [14784, 8192], P('col', 'row'), may hold values from -0.046875 to 0.046875
- grad_out: bfloat16 [2048, 8192], P('col', 'row'), may hold values from -1.5 to 1.5
Outputs:
- grad_in: bfloat16 [2048, 8192], P('col', 'row')
- grad_gate: bfloat16 [8192, 14784], P('row', 'col')
- grad_up: bfloat16 [8192, 14784], P('row', 'col')
- grad_down: bfloat16 [14784, 8192], P('col', 'row')
All inputs are finite; a program needn't handle non-finite values.
Results may differ from a plain program's by a relative error of at most 0.025.
Values may be sent and summed in bfloat16 or wider, within the bound.
No kernel may reach another device: no remote copies, remote signals or barrier semaphores. Data moves between devices by JAX's collectives and lax.ppermute only.
A program may use at most 64 MiB of HBM per device.

v0:
```python
import jax
import jax.numpy as jnp
from jax import lax
from jax.sharding import PartitionSpec as P


def contract_rows(left, right):
    return lax.dot_general(
        left, right, (((0,), (0,)), ((), ())), preferred_element_type=jnp.float32
    )


def contract_cols(left, right):
    return lax.dot_general(
        left, right, (((1,), (1,)), ((), ())), preferred_element_type=jnp.float32
    )


def pointwise(gate_pre, up_pre, hidden_grad):
    gate_value = gate_pre.astype(jnp.float32)
    up_value = up_pre.astype(jnp.float32)
    sigmoid_gate = jax.nn.sigmoid(gate_value)
    activated = gate_value * sigmoid_gate
    hidden = (activated * up_value).astype(jnp.bfloat16)
    up_grad = (hidden_grad * activated).astype(jnp.bfloat16)
    gate_grad = (
        hidden_grad * up_value * sigmoid_gate * (1.0 + gate_value * (1.0 - sigmoid_gate))
    ).astype(jnp.bfloat16)
    return (hidden, gate_grad, up_grad)


def _shifts(n):
    up = [(j, (j + 1) % n) for j in range(n)]
    down = [(j, (j - 1) % n) for j in range(n)]
    return (up, down)


def ring_all_gather(x, axis, n):
    me = lax.axis_index(axis)
    up, down = _shifts(n)
    n_up = n // 2
    n_down = n - 1 - n_up
    out = jnp.zeros((n,) + x.shape, x.dtype)
    out = lax.dynamic_update_index_in_dim(out, x, me, 0)
    a = x
    b = x
    for s in range(1, n_up + 1):
        a = lax.ppermute(a, axis, up)
        out = lax.dynamic_update_index_in_dim(out, a, (me - s + n) % n, 0)
        if s <= n_down:
            b = lax.ppermute(b, axis, down)
            out = lax.dynamic_update_index_in_dim(out, b, (me + s) % n, 0)
    return out


def ring_reduce_scatter(parts, axis, n, wire_dtype):
    me = lax.axis_index(axis)
    up, down = _shifts(n)
    n_up = n // 2
    n_down = n - 1 - n_up

    def block(j):
        return lax.dynamic_index_in_dim(parts, (j + 2 * n) % n, 0, keepdims=False).astype(
            jnp.float32
        )

    a = block(me + n_up)
    b = block(me - n_down)
    for s in range(n_up):
        a = lax.ppermute(a.astype(wire_dtype), axis, up).astype(jnp.float32)
        if s < n_up - 1:
            a = a + block(me + n_up - 1 - s)
        if s < n_down:
            b = lax.ppermute(b.astype(wire_dtype), axis, down).astype(jnp.float32)
            if s < n_down - 1:
                b = b + block(me - n_down + 1 + s)
    return block(me) + a + b


def shards(inputs, gate_pre, up_pre, w_gate, w_up, w_down, grad_out, n_row):
    tokens_row, hidden_units = gate_pre.shape
    pre = jnp.stack([gate_pre, up_pre], axis=1)
    all_pre = ring_all_gather(pre, "row", n_row).reshape((n_row * tokens_row, 2, hidden_units))
    all_grad_out = lax.all_gather(grad_out, "col", axis=0, tiled=True)
    all_inputs = lax.all_gather(inputs, "col", axis=0, tiled=True)
    part = contract_cols(all_grad_out, w_down).astype(jnp.bfloat16)
    part = part.reshape((n_row, tokens_row, hidden_units))
    own = ring_reduce_scatter(part, "row", n_row, jnp.bfloat16).astype(jnp.bfloat16)
    hidden_grad = ring_all_gather(own, "row", n_row).reshape((n_row * tokens_row, hidden_units))
    hidden, gate_grad, up_grad = pointwise(
        all_pre[:, 0], all_pre[:, 1], hidden_grad.astype(jnp.float32)
    )
    grad_down = contract_rows(hidden, all_grad_out).astype(jnp.bfloat16)
    grad_gate = contract_rows(all_inputs, gate_grad).astype(jnp.bfloat16)
    grad_up = contract_rows(all_inputs, up_grad).astype(jnp.bfloat16)
    grad_in = lax.psum_scatter(
        (contract_cols(gate_grad, w_gate) + contract_cols(up_grad, w_up)).astype(jnp.bfloat16),
        "col",
        scatter_dimension=0,
        tiled=True,
    )
    return (grad_in, grad_gate, grad_up, grad_down)


def solution(mesh):
    n_row = mesh.shape["row"]

    def body(*args):
        return shards(*args, n_row=n_row)

    return jax.shard_map(
        body,
        mesh=mesh,
        in_specs=(
            P("col", "row"),
            P("row", "col"),
            P("row", "col"),
            P("row", "col"),
            P("row", "col"),
            P("col", "row"),
            P("col", "row"),
        ),
        out_specs=(P("col", "row"), P("row", "col"), P("row", "col"), P("col", "row")),
        check_vma=False,
    )
```

profile of v0, /device:TPU:2, one launch (start us, length us, event | category | flops | bytes accessed | tf_op | source)
XLA Modules:
  0.0 708.0 jit_solution(4396758375819040371)
XLA Ops:
  12.8 9.5 %collective-permute-start.31 = (bf16[128,2,462]{0,2,1:T(8,128)(2,1)S(1)}, bf16[128,2,462]{0,2,1:T(8,128)(2,1)}, u32[]{:S(2)}, u32[]{:S(2)}) collective-permute-start(bf16[128,2,462]{0,2,1:T(8,128)(2,1)S(1)} %get-tuple-element.22), channel_id=1, source_target_pairs={{0,480},{32,0},{64,32},{96,64},{128,96},{160,128},{192,160},{224,1... | collective-permute-start | bytes 709640 | tf_op jit(solution)/shard_map/ppermute | solution.py:51
  28.3 5.1 collective-permute-start.33
  38.2 36.0 %all-gather.3.cloned.1.call-done = bf16[2048,512]{1,0:T(8,128)(2,1)} async-done(((bf16[64,512]{1,0:T(8,128)(2,1)}), bf16[2048,512]{1,0:T(8,128)(2,1)}) %all-gather.3.cloned.1.call-update) | async-done | bytes 2097168 | tf_op jit(solution)/shard_map/all_gather | solution.py:84
  101.7 5.1 collective-permute-start.9
  118.3 5.5 collective-permute-start.11
  126.3 5.5 collective-permute-start.12
  134.3 5.5 collective-permute-start.13
  142.3 5.6 collective-permute-start.14
  150.0 5.1 collective-permute-start.37
  182.6 5.6 collective-permute-start.20
  190.2 5.1 collective-permute-start.41
  204.8 5.5 collective-permute-start.24
  212.3 5.1 collective-permute-start.43
  219.4 5.1 collective-permute-start.26
  226.9 5.6 collective-permute-start.28
  237.7 14.5 %dynamic_update_slice.114 = bf16[16,128,2,462]{1,0,3,2:T(8,128)(2,1)} dynamic-update-slice(bf16[16,128,2,462]{1,0,3,2:T(8,128)(2,1)} %broadcast_in_dim.121, bf16[1,128,2,462]{1,0,3,2:T(2,128)(2,1)S(1)} %copy.56, s32[]{:T(128)S(6)} %select_n.304, s32[]{:T(128)} %constant.338.clone.1, s32[]{:T(128)} %constant.338.clone.1, s32[]{:T(128)} %constant.338.clone.1) | dynamic-update-slice | bytes 473092 | tf_op jit(solution)/shard_map/jit(dynamic_update_index_in_dim)/dynamic_update_slice | solution.py:44
  253.8 14.3 %dynamic_update_slice.115 = bf16[16,128,2,462]{1,0,3,2:T(8,128)(2,1)} dynamic-update-slice(bf16[16,128,2,462]{1,0,3,2:T(8,128)(2,1)} %dynamic_update_slice.114, bf16[1,128,2,462]{1,0,3,2:T(2,128)(2,1)S(1)} %copy.57, s32[]{:T(128)S(6)} %select_n.306, s32[]{:T(128)} %constant.338.clone.1, s32[]{:T(128)} %constant.338.clone.1, s32[]{:T(128)} %constant.338.clone.1) | dynamic-update-slice | bytes 473092 | tf_op jit(solution)/shard_map/jit(dynamic_update_index_in_dim)/dynamic_update_slice | solution.py:49
  268.1 14.3 %dynamic_update_slice.116 = bf16[16,128,2,462]{1,0,3,2:T(8,128)(2,1)} dynamic-update-slice(bf16[16,128,2,462]{1,0,3,2:T(8,128)(2,1)} %dynamic_update_slice.115, bf16[1,128,2,462]{1,0,3,2:T(2,128)(2,1)S(1)} %copy.58, s32[]{:T(128)S(6)} %select_n.308, s32[]{:T(128)} %constant.338.clone.1, s32[]{:T(128)} %constant.338.clone.1, s32[]{:T(128)} %constant.338.clone.1) | dynamic-update-slice | bytes 473092 | tf_op jit(solution)/shard_map/jit(dynamic_update_index_in_dim)/dynamic_update_slice | solution.py:52
  285.1 14.3 %dynamic_update_slice.117 = bf16[16,128,2,462]{1,0,3,2:T(8,128)(2,1)} dynamic-update-slice(bf16[16,128,2,462]{1,0,3,2:T(8,128)(2,1)} %dynamic_update_slice.116, bf16[1,128,2,462]{1,0,3,2:T(2,128)(2,1)S(1)} %copy.59, s32[]{:T(128)S(6)} %select_n.310, s32[]{:T(128)} %constant.338.clone.1, s32[]{:T(128)} %constant.338.clone.1, s32[]{:T(128)} %constant.338.clone.1) | dynamic-update-slice | bytes 473092 | tf_op jit(solution)/shard_map/jit(dynamic_update_index_in_dim)/dynamic_update_slice | solution.py:49
  299.4 14.3 %dynamic_update_slice.118 = bf16[16,128,2,462]{1,0,3,2:T(8,128)(2,1)} dynamic-update-slice(bf16[16,128,2,462]{1,0,3,2:T(8,128)(2,1)} %dynamic_update_slice.117, bf16[1,128,2,462]{1,0,3,2:T(2,128)(2,1)S(1)} %copy.60, s32[]{:T(128)S(6)} %select_n.312, s32[]{:T(128)} %constant.338.clone.1, s32[]{:T(128)} %constant.338.clone.1, s32[]{:T(128)} %constant.338.clone.1) | dynamic-update-slice | bytes 473092 | tf_op jit(solution)/shard_map/jit(dynamic_update_index_in_dim)/dynamic_update_slice | solution.py:52
  315.4 14.3 %dynamic_update_slice.119 = bf16[16,128,2,462]{1,0,3,2:T(8,128)(2,1)} dynamic-update-slice(bf16[16,128,2,462]{1,0,3,2:T(8,128)(2,1)} %dynamic_update_slice.118, bf16[1,128,2,462]{1,0,3,2:T(2,128)(2,1)S(1)} %copy.61, s32[]{:T(128)S(6)} %select_n.314, s32[]{:T(128)} %constant.338.clone.1, s32[]{:T(128)} %constant.338.clone.1, s32[]{:T(128)} %constant.338.clone.1) | dynamic-update-slice | bytes 473092 | tf_op jit(solution)/shard_map/jit(dynamic_update_index_in_dim)/dynamic_update_slice | solution.py:49
  329.7 14.3 %dynamic_update_slice.120 = bf16[16,128,2,462]{1,0,3,2:T(8,128)(2,1)} dynamic-update-slice(bf16[16,128,2,462]{1,0,3,2:T(8,128)(2,1)} %dynamic_update_slice.119, bf16[1,128,2,462]{1,0,3,2:T(2,128)(2,1)S(1)} %copy.62, s32[]{:T(128)S(6)} %select_n.316, s32[]{:T(128)} %constant.338.clone.1, s32[]{:T(128)} %constant.338.clone.1, s32[]{:T(128)} %constant.338.clone.1) | dynamic-update-slice | bytes 473092 | tf_op jit(solution)/shard_map/jit(dynamic_update_index_in_dim)/dynamic_update_slice | solution.py:52
  344.7 14.3 %dynamic_update_slice.121 = bf16[16,128,2,462]{1,0,3,2:T(8,128)(2,1)} dynamic-update-slice(bf16[16,128,2,462]{1,0,3,2:T(8,128)(2,1)} %dynamic_update_slice.120, bf16[1,128,2,462]{1,0,3,2:T(2,128)(2,1)S(1)} %copy.63, s32[]{:T(128)S(6)} %select_n.318, s32[]{:T(128)} %constant.338.clone.1, s32[]{:T(128)} %constant.338.clone.1, s32[]{:T(128)} %constant.338.clone.1) | dynamic-update-slice | bytes 473092 | tf_op jit(solution)/shard_map/jit(dynamic_update_index_in_dim)/dynamic_update_slice | solution.py:49
  359.0 14.3 %dynamic_update_slice.122 = bf16[16,128,2,462]{1,0,3,2:T(8,128)(2,1)} dynamic-update-slice(bf16[16,128,2,462]{1,0,3,2:T(8,128)(2,1)} %dynamic_update_slice.121, bf16[1,128,2,462]{1,0,3,2:T(2,128)(2,1)S(1)} %copy.64, s32[]{:T(128)S(6)} %select_n.320, s32[]{:T(128)} %constant.338.clone.1, s32[]{:T(128)} %constant.338.clone.1, s32[]{:T(128)} %constant.338.clone.1) | dynamic-update-slice | bytes 473092 | tf_op jit(solution)/shard_map/jit(dynamic_update_index_in_dim)/dynamic_update_slice | solution.py:52
  374.0 14.3 %dynamic_update_slice.123 = bf16[16,128,2,462]{1,0,3,2:T(8,128)(2,1)} dynamic-update-slice(bf16[16,128,2,462]{1,0,3,2:T(8,128)(2,1)} %dynamic_update_slice.122, bf16[1,128,2,462]{1,0,3,2:T(2,128)(2,1)S(1)} %copy.65, s32[]{:T(128)S(6)} %select_n.322, s32[]{:T(128)} %constant.338.clone.1, s32[]{:T(128)} %constant.338.clone.1, s32[]{:T(128)} %constant.338.clone.1) | dynamic-update-slice | bytes 473092 | tf_op jit(solution)/shard_map/jit(dynamic_update_index_in_dim)/dynamic_update_slice | solution.py:49
  388.3 14.3 %dynamic_update_slice.124 = bf16[16,128,2,462]{1,0,3,2:T(8,128)(2,1)} dynamic-update-slice(bf16[16,128,2,462]{1,0,3,2:T(8,128)(2,1)} %dynamic_update_slice.123, bf16[1,128,2,462]{1,0,3,2:T(2,128)(2,1)S(1)} %copy.66, s32[]{:T(128)S(6)} %select_n.324, s32[]{:T(128)} %constant.338.clone.1, s32[]{:T(128)} %constant.338.clone.1, s32[]{:T(128)} %constant.338.clone.1) | dynamic-update-slice | bytes 473092 | tf_op jit(solution)/shard_map/jit(dynamic_update_index_in_dim)/dynamic_update_slice | solution.py:52
  403.3 14.5 %dynamic_update_slice.125 = bf16[16,128,2,462]{1,0,3,2:T(8,128)(2,1)} dynamic-update-slice(bf16[16,128,2,462]{1,0,3,2:T(8,128)(2,1)} %dynamic_update_slice.124, bf16[1,128,2,462]{1,0,3,2:T(2,128)(2,1)S(1)} %copy.67, s32[]{:T(128)S(6)} %select_n.326, s32[]{:T(128)} %constant.338.clone.1, s32[]{:T(128)} %constant.338.clone.1, s32[]{:T(128)} %constant.338.clone.1) | dynamic-update-slice | bytes 473092 | tf_op jit(solution)/shard_map/jit(dynamic_update_index_in_dim)/dynamic_update_slice | solution.py:49
  417.9 14.3 %dynamic_update_slice.126 = bf16[16,128,2,462]{1,0,3,2:T(8,128)(2,1)} dynamic-update-slice(bf16[16,128,2,462]{1,0,3,2:T(8,128)(2,1)} %dynamic_update_slice.125, bf16[1,128,2,462]{1,0,3,2:T(2,128)(2,1)S(1)} %copy.68, s32[]{:T(128)S(6)} %select_n.328, s32[]{:T(128)} %constant.338.clone.1, s32[]{:T(128)} %constant.338.clone.1, s32[]{:T(128)} %constant.338.clone.1) | dynamic-update-slice | bytes 473092 | tf_op jit(solution)/shard_map/jit(dynamic_update_index_in_dim)/dynamic_update_slice | solution.py:52
  433.8 14.3 %dynamic_update_slice.127 = bf16[16,128,2,462]{1,0,3,2:T(8,128)(2,1)} dynamic-update-slice(bf16[16,128,2,462]{1,0,3,2:T(8,128)(2,1)} %dynamic_update_slice.126, bf16[1,128,2,462]{1,0,3,2:T(2,128)(2,1)S(1)} %copy.69, s32[]{:T(128)S(6)} %select_n.330, s32[]{:T(128)} %constant.338.clone.1, s32[]{:T(128)} %constant.338.clone.1, s32[]{:T(128)} %constant.338.clone.1) | dynamic-update-slice | bytes 473092 | tf_op jit(solution)/shard_map/jit(dynamic_update_index_in_dim)/dynamic_update_slice | solution.py:49
  448.1 14.3 %dynamic_update_slice.128 = bf16[16,128,2,462]{1,0,3,2:T(8,128)(2,1)} dynamic-update-slice(bf16[16,128,2,462]{1,0,3,2:T(8,128)(2,1)} %dynamic_update_slice.127, bf16[1,128,2,462]{1,0,3,2:T(2,128)(2,1)S(1)} %copy.70, s32[]{:T(128)S(6)} %select_n.332, s32[]{:T(128)} %constant.338.clone.1, s32[]{:T(128)} %constant.338.clone.1, s32[]{:T(128)} %constant.338.clone.1) | dynamic-update-slice | bytes 473092 | tf_op jit(solution)/shard_map/jit(dynamic_update_index_in_dim)/dynamic_update_slice | solution.py:52
  463.7 14.3 %dynamic_update_slice.129 = bf16[16,128,2,462]{1,0,3,2:T(8,128)(2,1)} dynamic-update-slice(bf16[16,128,2,462]{1,0,3,2:T(8,128)(2,1)} %dynamic_update_slice.128, bf16[1,128,2,462]{1,0,3,2:T(2,128)(2,1)S(1)} %copy.71, s32[]{:T(128)S(6)} %select_n.334, s32[]{:T(128)} %constant.338.clone.1, s32[]{:T(128)} %constant.338.clone.1, s32[]{:T(128)} %constant.338.clone.1) | dynamic-update-slice | bytes 473092 | tf_op jit(solution)/shard_map/jit(dynamic_update_index_in_dim)/dynamic_update_slice | solution.py:49
  483.0 6.2 dynamic_update_slice.98
  489.6 6.2 dynamic_update_slice.99
  495.7 6.2 dynamic_update_slice.100
  502.3 6.2 dynamic_update_slice.101
  508.5 6.2 dynamic_update_slice.102
  515.0 6.2 dynamic_update_slice.103
  521.2 6.2 dynamic_update_slice.104
  527.8 6.6 dynamic_update_slice.105
  534.3 6.2 dynamic_update_slice.106
  540.9 6.2 dynamic_update_slice.107
  547.0 6.2 dynamic_update_slice.108
  554.5 6.2 dynamic_update_slice.109
  560.7 6.2 dynamic_update_slice.110
  569.0 6.2 dynamic_update_slice.111
  575.2 6.2 dynamic_update_slice.112
  582.4 6.2 dynamic_update_slice.113
  607.8 93.5 %reduce-scatter.2.cloned.1.call-done = bf16[64,512]{1,0:T(8,128)(2,1)} async-done(((bf16[2048,512]{1,0:T(8,128)(2,1)}), bf16[64,512]{1,0:T(8,128)(2,1)}) %reduce-scatter.2.cloned.1.call-update) | async-done | bytes 65552 | tf_op jit(solution)/shard_map/reduce_scatter | solution.py:96
  (216 shorter events, 155.5 us)
Async XLA Ops:
  7.2 67.0 %all-gather.3.cloned.1.call-start = ((), (), s32[]{:S(2)}) async-start(), calls=%async_computation.1 | async-start | bytes 2162688 | tf_op jit(solution)/shard_map/all_gather | solution.py:84
  7.9 594.3 %all-gather.5.cloned.1.call-start = ((), (), s32[]{:S(2)}) async-start(), calls=%async_computation.3 | async-start | bytes 2162688 | tf_op jit(solution)/shard_map/all_gather | solution.py:85
  9.0 17.2 %collective-permute-start.30 = (bf16[128,2,462]{0,2,1:T(8,128)(2,1)S(1)}, bf16[128,2,462]{0,2,1:T(8,128)(2,1)S(1)}, u32[]{:S(2)}, u32[]{:S(2)}) collective-permute-start(bf16[128,2,462]{0,2,1:T(8,128)(2,1)S(1)} %get-tuple-element.22), channel_id=1, source_target_pairs={{0,32},{32,64},{64,96},{96,128},{128,160},{160,192},{192,224},{224... | collective-permute-start | bytes 709640 | tf_op jit(solution)/shard_map/ppermute | solution.py:48
  12.8 15.5 %collective-permute-start.31 = (bf16[128,2,462]{0,2,1:T(8,128)(2,1)S(1)}, bf16[128,2,462]{0,2,1:T(8,128)(2,1)}, u32[]{:S(2)}, u32[]{:S(2)}) collective-permute-start(bf16[128,2,462]{0,2,1:T(8,128)(2,1)S(1)} %get-tuple-element.22), channel_id=1, source_target_pairs={{0,480},{32,0},{64,32},{96,64},{128,96},{160,128},{192,160},{224,1... | collective-permute-start | bytes 709640 | tf_op jit(solution)/shard_map/ppermute | solution.py:51
  26.1 10.1 %collective-permute-start.32 = (bf16[128,2,462]{0,2,1:T(8,128)(2,1)S(1)}, bf16[128,2,462]{0,2,1:T(8,128)(2,1)}, u32[]{:S(2)}, u32[]{:S(2)}) collective-permute-start(bf16[128,2,462]{0,2,1:T(8,128)(2,1)S(1)} %collective-permute-done.30), channel_id=1, source_target_pairs={{0,32},{32,64},{64,96},{96,128},{128,160},{160,192},{192,224},{224... | collective-permute-start | bytes 709640 | tf_op jit(solution)/shard_map/ppermute | solution.py:48
  28.3 58.0 %collective-permute-start.33 = (bf16[128,2,462]{0,2,1:T(8,128)(2,1)}, bf16[128,2,462]{0,2,1:T(8,128)(2,1)}, u32[]{:S(2)}, u32[]{:S(2)}) collective-permute-start(bf16[128,2,462]{0,2,1:T(8,128)(2,1)} %collective-permute-done.31), channel_id=1, source_target_pairs={{0,480},{32,0},{64,32},{96,64},{128,96},{160,128},{192,160},{224,1... | collective-permute-start | bytes 709640 | tf_op jit(solution)/shard_map/ppermute | solution.py:51
  36.3 54.4 %collective-permute-start.34 = (bf16[128,2,462]{0,2,1:T(8,128)(2,1)}, bf16[128,2,462]{0,2,1:T(8,128)(2,1)}, u32[]{:S(2)}, u32[]{:S(2)}) collective-permute-start(bf16[128,2,462]{0,2,1:T(8,128)(2,1)} %collective-permute-done.32), channel_id=1, source_target_pairs={{0,32},{32,64},{64,96},{96,128},{128,160},{160,192},{192,224},{224... | collective-permute-start | bytes 709640 | tf_op jit(solution)/shard_map/ppermute | solution.py:48
  82.7 15.1 %collective-permute-start = (bf16[128,462]{0,1:T(8,128)(2,1)S(1)}, bf16[128,462]{0,1:T(8,128)(2,1)}, u32[]{:S(2)}, u32[]{:S(2)}) collective-permute-start(bf16[128,462]{0,1:T(8,128)(2,1)S(1)} %bitcast.191), channel_id=1, source_target_pairs={{0,32},{32,64},{64,96},{96,128},{128,160},{160,192},{192,224},{224... | collective-permute-start | bytes 354824 | tf_op jit(solution)/shard_map/ppermute | solution.py:70
  86.2 615.1 %reduce-scatter.2.cloned.1.call-start = ((), (), s32[]{:S(2)}) async-start(), calls=%async_computation.2 | async-start | bytes 2162688 | tf_op jit(solution)/shard_map/reduce_scatter | solution.py:96
  86.3 63.7 %collective-permute-start.35 = (bf16[128,2,462]{0,2,1:T(8,128)(2,1)}, bf16[128,2,462]{0,2,1:T(8,128)(2,1)S(1)}, u32[]{:S(2)}, u32[]{:S(2)}) collective-permute-start(bf16[128,2,462]{0,2,1:T(8,128)(2,1)} %collective-permute-done.33), channel_id=1, source_target_pairs={{0,480},{32,0},{64,32},{96,64},{128,96},{160,128},{192,160},{224,1... | collective-permute-start | bytes 709640 | tf_op jit(solution)/shard_map/ppermute | solution.py:51
  90.7 64.4 %collective-permute-start.36 = (bf16[128,2,462]{0,2,1:T(8,128)(2,1)}, bf16[128,2,462]{0,2,1:T(8,128)(2,1)S(1)}, u32[]{:S(2)}, u32[]{:S(2)}) collective-permute-start(bf16[128,2,462]{0,2,1:T(8,128)(2,1)} %collective-permute-done.34), channel_id=1, source_target_pairs={{0,32},{32,64},{64,96},{96,128},{128,160},{160,192},{192,224},{224... | collective-permute-start | bytes 709640 | tf_op jit(solution)/shard_map/ppermute | solution.py:48
  92.6 8.1 %collective-permute-start.8 = (bf16[128,462]{0,1:T(8,128)(2,1)S(1)}, bf16[128,462]{0,1:T(8,128)(2,1)S(1)}, u32[]{:S(2)}, u32[]{:S(2)}) collective-permute-start(bf16[128,462]{0,1:T(8,128)(2,1)S(1)} %bitcast.192), channel_id=1, source_target_pairs={{0,480},{32,0},{64,32},{96,64},{128,96},{160,128},{192,160},{224,1... | collective-permute-start | bytes 354824 | tf_op jit(solution)/shard_map/ppermute | solution.py:74
  98.8 8.1 %collective-permute-start.1 = (bf16[128,462]{0,1:T(8,128)(2,1)S(1)}, bf16[128,462]{0,1:T(8,128)(2,1)S(1)}, u32[]{:S(2)}, u32[]{:S(2)}) collective-permute-start(bf16[128,462]{0,1:T(8,128)(2,1)S(1)} %fusion.27), channel_id=1, source_target_pairs={{0,32},{32,64},{64,96},{96,128},{128,160},{160,192},{192,224},{224... | collective-permute-start | bytes 354824 | tf_op jit(solution)/shard_map/ppermute | solution.py:70
  101.7 8.1 %collective-permute-start.9 = (bf16[128,462]{0,1:T(8,128)(2,1)S(1)}, bf16[128,462]{0,1:T(8,128)(2,1)S(1)}, u32[]{:S(2)}, u32[]{:S(2)}) collective-permute-start(bf16[128,462]{0,1:T(8,128)(2,1)S(1)} %fusion.20), channel_id=1, source_target_pairs={{0,480},{32,0},{64,32},{96,64},{128,96},{160,128},{192,160},{224,1... | collective-permute-start | bytes 354824 | tf_op jit(solution)/shard_map/ppermute | solution.py:74
  107.9 8.1 %collective-permute-start.2 = (bf16[128,462]{0,1:T(8,128)(2,1)S(1)}, bf16[128,462]{0,1:T(8,128)(2,1)S(1)}, u32[]{:S(2)}, u32[]{:S(2)}) collective-permute-start(bf16[128,462]{0,1:T(8,128)(2,1)S(1)} %fusion.26), channel_id=1, source_target_pairs={{0,32},{32,64},{64,96},{96,128},{128,160},{160,192},{192,224},{224... | collective-permute-start | bytes 354824 | tf_op jit(solution)/shard_map/ppermute | solution.py:70
  110.8 7.5 %collective-permute-start.10 = (bf16[128,462]{0,1:T(8,128)(2,1)S(1)}, bf16[128,462]{0,1:T(8,128)(2,1)S(1)}, u32[]{:S(2)}, u32[]{:S(2)}) collective-permute-start(bf16[128,462]{0,1:T(8,128)(2,1)S(1)} %fusion.19), channel_id=1, source_target_pairs={{0,480},{32,0},{64,32},{96,64},{128,96},{160,128},{192,160},{224,1... | collective-permute-start | bytes 354824 | tf_op jit(solution)/shard_map/ppermute | solution.py:74
  116.0 7.9 %collective-permute-start.3 = (bf16[128,462]{0,1:T(8,128)(2,1)S(1)}, bf16[128,462]{0,1:T(8,128)(2,1)S(1)}, u32[]{:S(2)}, u32[]{:S(2)}) collective-permute-start(bf16[128,462]{0,1:T(8,128)(2,1)S(1)} %fusion.25), channel_id=1, source_target_pairs={{0,32},{32,64},{64,96},{96,128},{128,160},{160,192},{192,224},{224... | collective-permute-start | bytes 354824 | tf_op jit(solution)/shard_map/ppermute | solution.py:70
  118.3 7.9 %collective-permute-start.11 = (bf16[128,462]{0,1:T(8,128)(2,1)S(1)}, bf16[128,462]{0,1:T(8,128)(2,1)S(1)}, u32[]{:S(2)}, u32[]{:S(2)}) collective-permute-start(bf16[128,462]{0,1:T(8,128)(2,1)S(1)} %fusion.18), channel_id=1, source_target_pairs={{0,480},{32,0},{64,32},{96,64},{128,96},{160,128},{192,160},{224,1... | collective-permute-start | bytes 354824 | tf_op jit(solution)/shard_map/ppermute | solution.py:74
  124.0 7.9 %collective-permute-start.4 = (bf16[128,462]{0,1:T(8,128)(2,1)S(1)}, bf16[128,462]{0,1:T(8,128)(2,1)S(1)}, u32[]{:S(2)}, u32[]{:S(2)}) collective-permute-start(bf16[128,462]{0,1:T(8,128)(2,1)S(1)} %fusion.24), channel_id=1, source_target_pairs={{0,32},{32,64},{64,96},{96,128},{128,160},{160,192},{192,224},{224... | collective-permute-start | bytes 354824 | tf_op jit(solution)/shard_map/ppermute | solution.py:70
  126.3 7.9 %collective-permute-start.12 = (bf16[128,462]{0,1:T(8,128)(2,1)S(1)}, bf16[128,462]{0,1:T(8,128)(2,1)S(1)}, u32[]{:S(2)}, u32[]{:S(2)}) collective-permute-start(bf16[128,462]{0,1:T(8,128)(2,1)S(1)} %fusion.17), channel_id=1, source_target_pairs={{0,480},{32,0},{64,32},{96,64},{128,96},{160,128},{192,160},{224,1... | collective-permute-start | bytes 354824 | tf_op jit(solution)/shard_map/ppermute | solution.py:74
  131.9 7.9 %collective-permute-start.5 = (bf16[128,462]{0,1:T(8,128)(2,1)S(1)}, bf16[128,462]{0,1:T(8,128)(2,1)S(1)}, u32[]{:S(2)}, u32[]{:S(2)}) collective-permute-start(bf16[128,462]{0,1:T(8,128)(2,1)S(1)} %fusion.23), channel_id=1, source_target_pairs={{0,32},{32,64},{64,96},{96,128},{128,160},{160,192},{192,224},{224... | collective-permute-start | bytes 354824 | tf_op jit(solution)/shard_map/ppermute | solution.py:70
  134.3 8.0 %collective-permute-start.13 = (bf16[128,462]{0,1:T(8,128)(2,1)S(1)}, bf16[128,462]{0,1:T(8,128)(2,1)S(1)}, u32[]{:S(2)}, u32[]{:S(2)}) collective-permute-start(bf16[128,462]{0,1:T(8,128)(2,1)S(1)} %fusion.16), channel_id=1, source_target_pairs={{0,480},{32,0},{64,32},{96,64},{128,96},{160,128},{192,160},{224,1... | collective-permute-start | bytes 354824 | tf_op jit(solution)/shard_map/ppermute | solution.py:74
  139.9 8.0 %collective-permute-start.6 = (bf16[128,462]{0,1:T(8,128)(2,1)S(1)}, bf16[128,462]{0,1:T(8,128)(2,1)S(1)}, u32[]{:S(2)}, u32[]{:S(2)}) collective-permute-start(bf16[128,462]{0,1:T(8,128)(2,1)S(1)} %fusion.22), channel_id=1, source_target_pairs={{0,32},{32,64},{64,96},{96,128},{128,160},{160,192},{192,224},{224... | collective-permute-start | bytes 354824 | tf_op jit(solution)/shard_map/ppermute | solution.py:70
  142.3 14.7 %collective-permute-start.14 = (bf16[128,462]{0,1:T(8,128)(2,1)S(1)}, bf16[128,462]{0,1:T(8,128)(2,1)S(1)}, u32[]{:S(2)}, u32[]{:S(2)}) collective-permute-start(bf16[128,462]{0,1:T(8,128)(2,1)S(1)} %fusion.15), channel_id=1, source_target_pairs={{0,480},{32,0},{64,32},{96,64},{128,96},{160,128},{192,160},{224,1... | collective-permute-start | bytes 354824 | tf_op jit(solution)/shard_map/ppermute | solution.py:74
  148.0 9.2 %collective-permute-start.7 = (bf16[128,462]{0,1:T(8,128)(2,1)S(1)}, bf16[128,462]{0,1:T(8,128)(2,1)S(1)}, u32[]{:S(2)}, u32[]{:S(2)}) collective-permute-start(bf16[128,462]{0,1:T(8,128)(2,1)S(1)} %fusion.21), channel_id=1, source_target_pairs={{0,32},{32,64},{64,96},{96,128},{128,160},{160,192},{192,224},{224... | collective-permute-start | bytes 354824 | tf_op jit(solution)/shard_map/ppermute | solution.py:70
  150.0 18.0 %collective-permute-start.37 = (bf16[128,2,462]{0,2,1:T(8,128)(2,1)S(1)}, bf16[128,2,462]{0,2,1:T(8,128)(2,1)S(1)}, u32[]{:S(2)}, u32[]{:S(2)}) collective-permute-start(bf16[128,2,462]{0,2,1:T(8,128)(2,1)S(1)} %collective-permute-done.35), channel_id=1, source_target_pairs={{0,480},{32,0},{64,32},{96,64},{128,96},{160,128},{192,160},{224,1... | collective-permute-start | bytes 709640 | tf_op jit(solution)/shard_map/ppermute | solution.py:51
  155.1 18.0 %collective-permute-start.38 = (bf16[128,2,462]{0,2,1:T(8,128)(2,1)S(1)}, bf16[128,2,462]{0,2,1:T(8,128)(2,1)S(1)}, u32[]{:S(2)}, u32[]{:S(2)}) collective-permute-start(bf16[128,2,462]{0,2,1:T(8,128)(2,1)S(1)} %collective-permute-done.36), channel_id=1, source_target_pairs={{0,32},{32,64},{64,96},{96,128},{128,160},{160,192},{192,224},{224... | collective-permute-start | bytes 709640 | tf_op jit(solution)/shard_map/ppermute | solution.py:48
  157.3 8.8 %collective-permute-start.15 = (bf16[128,462]{0,1:T(8,128)(2,1)S(1)}, bf16[128,462]{0,1:T(8,128)(2,1)S(1)}, u32[]{:S(2)}, u32[]{:S(2)}) collective-permute-start(bf16[128,462]{0,1:T(8,128)(2,1)S(1)} %fusion.29), channel_id=1, source_target_pairs={{0,32},{32,64},{64,96},{96,128},{128,160},{160,192},{192,224},{224... | collective-permute-start | bytes 354824 | tf_op jit(solution)/shard_map/ppermute | solution.py:48
  159.5 15.6 %collective-permute-start.16 = (bf16[128,462]{0,1:T(8,128)(2,1)S(1)}, bf16[128,462]{0,1:T(8,128)(2,1)S(1)}, u32[]{:S(2)}, u32[]{:S(2)}) collective-permute-start(bf16[128,462]{0,1:T(8,128)(2,1)S(1)} %fusion.29), channel_id=1, source_target_pairs={{0,480},{32,0},{64,32},{96,64},{128,96},{160,128},{192,160},{224,1... | collective-permute-start | bytes 354824 | tf_op jit(solution)/shard_map/ppermute | solution.py:51
  166.0 14.2 %collective-permute-start.17 = (bf16[128,462]{0,1:T(8,128)(2,1)S(1)}, bf16[128,462]{0,1:T(8,128)(2,1)S(1)}, u32[]{:S(2)}, u32[]{:S(2)}) collective-permute-start(bf16[128,462]{0,1:T(8,128)(2,1)S(1)} %collective-permute-done.15), channel_id=1, source_target_pairs={{0,32},{32,64},{64,96},{96,128},{128,160},{160,192},{192,224},{224... | collective-permute-start | bytes 354824 | tf_op jit(solution)/shard_map/ppermute | solution.py:48
  168.0 22.2 %collective-permute-start.39 = (bf16[128,2,462]{0,2,1:T(8,128)(2,1)S(1)}, bf16[128,2,462]{0,2,1:T(8,128)(2,1)S(1)}, u32[]{:S(2)}, u32[]{:S(2)}) collective-permute-start(bf16[128,2,462]{0,2,1:T(8,128)(2,1)S(1)} %collective-permute-done.37), channel_id=1, source_target_pairs={{0,480},{32,0},{64,32},{96,64},{128,96},{160,128},{192,160},{224,1... | collective-permute-start | bytes 709640 | tf_op jit(solution)/shard_map/ppermute | solution.py:51
  173.1 22.2 %collective-permute-start.40 = (bf16[128,2,462]{0,2,1:T(8,128)(2,1)S(1)}, bf16[128,2,462]{0,2,1:T(8,128)(2,1)S(1)}, u32[]{:S(2)}, u32[]{:S(2)}) collective-permute-start(bf16[128,2,462]{0,2,1:T(8,128)(2,1)S(1)} %collective-permute-done.38), channel_id=1, source_target_pairs={{0,32},{32,64},{64,96},{96,128},{128,160},{160,192},{192,224},{224... | collective-permute-start | bytes 709640 | tf_op jit(solution)/shard_map/ppermute | solution.py:48
  175.1 7.5 %collective-permute-start.18 = (bf16[128,462]{0,1:T(8,128)(2,1)S(1)}, bf16[128,462]{0,1:T(8,128)(2,1)S(1)}, u32[]{:S(2)}, u32[]{:S(2)}) collective-permute-start(bf16[128,462]{0,1:T(8,128)(2,1)S(1)} %collective-permute-done.16), channel_id=1, source_target_pairs={{0,480},{32,0},{64,32},{96,64},{128,96},{160,128},{192,160},{224,1... | collective-permute-start | bytes 354824 | tf_op jit(solution)/shard_map/ppermute | solution.py:51
  180.2 8.0 %collective-permute-start.19 = (bf16[128,462]{0,1:T(8,128)(2,1)S(1)}, bf16[128,462]{0,1:T(8,128)(2,1)S(1)}, u32[]{:S(2)}, u32[]{:S(2)}) collective-permute-start(bf16[128,462]{0,1:T(8,128)(2,1)S(1)} %collective-permute-done.17), channel_id=1, source_target_pairs={{0,32},{32,64},{64,96},{96,128},{128,160},{160,192},{192,224},{224... | collective-permute-start | bytes 354824 | tf_op jit(solution)/shard_map/ppermute | solution.py:48
  182.6 14.6 %collective-permute-start.20 = (bf16[128,462]{0,1:T(8,128)(2,1)S(1)}, bf16[128,462]{0,1:T(8,128)(2,1)S(1)}, u32[]{:S(2)}, u32[]{:S(2)}) collective-permute-start(bf16[128,462]{0,1:T(8,128)(2,1)S(1)} %collective-permute-done.18), channel_id=1, source_target_pairs={{0,480},{32,0},{64,32},{96,64},{128,96},{160,128},{192,160},{224,1... | collective-permute-start | bytes 354824 | tf_op jit(solution)/shard_map/ppermute | solution.py:51
  188.2 14.2 %collective-permute-start.21 = (bf16[128,462]{0,1:T(8,128)(2,1)S(1)}, bf16[128,462]{0,1:T(8,128)(2,1)S(1)}, u32[]{:S(2)}, u32[]{:S(2)}) collective-permute-start(bf16[128,462]{0,1:T(8,128)(2,1)S(1)} %collective-permute-done.19), channel_id=1, source_target_pairs={{0,32},{32,64},{64,96},{96,128},{128,160},{160,192},{192,224},{224... | collective-permute-start | bytes 354824 | tf_op jit(solution)/shard_map/ppermute | solution.py:48
  190.2 22.1 %collective-permute-start.41 = (bf16[128,2,462]{0,2,1:T(8,128)(2,1)S(1)}, bf16[128,2,462]{0,2,1:T(8,128)(2,1)S(1)}, u32[]{:S(2)}, u32[]{:S(2)}) collective-permute-start(bf16[128,2,462]{0,2,1:T(8,128)(2,1)S(1)} %collective-permute-done.39), channel_id=1, source_target_pairs={{0,480},{32,0},{64,32},{96,64},{128,96},{160,128},{192,160},{224,1... | collective-permute-start | bytes 709640 | tf_op jit(solution)/shard_map/ppermute | solution.py:51
  195.3 22.1 %collective-permute-start.42 = (bf16[128,2,462]{0,2,1:T(8,128)(2,1)S(1)}, bf16[128,2,462]{0,2,1:T(8,128)(2,1)S(1)}, u32[]{:S(2)}, u32[]{:S(2)}) collective-permute-start(bf16[128,2,462]{0,2,1:T(8,128)(2,1)S(1)} %collective-permute-done.40), channel_id=1, source_target_pairs={{0,32},{32,64},{64,96},{96,128},{128,160},{160,192},{192,224},{224... | collective-permute-start | bytes 709640 | tf_op jit(solution)/shard_map/ppermute | solution.py:48
  197.3 7.5 %collective-permute-start.22 = (bf16[128,462]{0,1:T(8,128)(2,1)S(1)}, bf16[128,462]{0,1:T(8,128)(2,1)S(1)}, u32[]{:S(2)}, u32[]{:S(2)}) collective-permute-start(bf16[128,462]{0,1:T(8,128)(2,1)S(1)} %collective-permute-done.20), channel_id=1, source_target_pairs={{0,480},{32,0},{64,32},{96,64},{128,96},{160,128},{192,160},{224,1... | collective-permute-start | bytes 354824 | tf_op jit(solution)/shard_map/ppermute | solution.py:51
  202.4 7.9 %collective-permute-start.23 = (bf16[128,462]{0,1:T(8,128)(2,1)S(1)}, bf16[128,462]{0,1:T(8,128)(2,1)S(1)}, u32[]{:S(2)}, u32[]{:S(2)}) collective-permute-start(bf16[128,462]{0,1:T(8,128)(2,1)S(1)} %collective-permute-done.21), channel_id=1, source_target_pairs={{0,32},{32,64},{64,96},{96,128},{128,160},{160,192},{192,224},{224... | collective-permute-start | bytes 354824 | tf_op jit(solution)/shard_map/ppermute | solution.py:48
  204.8 14.6 %collective-permute-start.24 = (bf16[128,462]{0,1:T(8,128)(2,1)S(1)}, bf16[128,462]{0,1:T(8,128)(2,1)S(1)}, u32[]{:S(2)}, u32[]{:S(2)}) collective-permute-start(bf16[128,462]{0,1:T(8,128)(2,1)S(1)} %collective-permute-done.22), channel_id=1, source_target_pairs={{0,480},{32,0},{64,32},{96,64},{128,96},{160,128},{192,160},{224,1... | collective-permute-start | bytes 354824 | tf_op jit(solution)/shard_map/ppermute | solution.py:51
  210.4 14.2 %collective-permute-start.25 = (bf16[128,462]{0,1:T(8,128)(2,1)S(1)}, bf16[128,462]{0,1:T(8,128)(2,1)S(1)}, u32[]{:S(2)}, u32[]{:S(2)}) collective-permute-start(bf16[128,462]{0,1:T(8,128)(2,1)S(1)} %collective-permute-done.23), channel_id=1, source_target_pairs={{0,32},{32,64},{64,96},{96,128},{128,160},{160,192},{192,224},{224... | collective-permute-start | bytes 354824 | tf_op jit(solution)/shard_map/ppermute | solution.py:48
  212.3 220.2 %collective-permute-start.43 = (bf16[128,2,462]{0,2,1:T(8,128)(2,1)S(1)}, bf16[128,2,462]{0,2,1:T(8,128)(2,1)}, u32[]{:S(2)}, u32[]{:S(2)}) collective-permute-start(bf16[128,2,462]{0,2,1:T(8,128)(2,1)S(1)} %collective-permute-done.41), channel_id=1, source_target_pairs={{0,480},{32,0},{64,32},{96,64},{128,96},{160,128},{192,160},{224,1... | collective-permute-start | bytes 709640 | tf_op jit(solution)/shard_map/ppermute | solution.py:51
  217.4 245.0 %collective-permute-start.44 = (bf16[128,2,462]{0,2,1:T(8,128)(2,1)S(1)}, bf16[128,2,462]{0,2,1:T(8,128)(2,1)}, u32[]{:S(2)}, u32[]{:S(2)}) collective-permute-start(bf16[128,2,462]{0,2,1:T(8,128)(2,1)S(1)} %collective-permute-done.42), channel_id=1, source_target_pairs={{0,32},{32,64},{64,96},{96,128},{128,160},{160,192},{192,224},{224... | collective-permute-start | bytes 709640 | tf_op jit(solution)/shard_map/ppermute | solution.py:48
  219.4 7.5 %collective-permute-start.26 = (bf16[128,462]{0,1:T(8,128)(2,1)S(1)}, bf16[128,462]{0,1:T(8,128)(2,1)}, u32[]{:S(2)}, u32[]{:S(2)}) collective-permute-start(bf16[128,462]{0,1:T(8,128)(2,1)S(1)} %collective-permute-done.24), channel_id=1, source_target_pairs={{0,480},{32,0},{64,32},{96,64},{128,96},{160,128},{192,160},{224,1... | collective-permute-start | bytes 354824 | tf_op jit(solution)/shard_map/ppermute | solution.py:51
  224.5 8.0 %collective-permute-start.27 = (bf16[128,462]{0,1:T(8,128)(2,1)S(1)}, bf16[128,462]{0,1:T(8,128)(2,1)}, u32[]{:S(2)}, u32[]{:S(2)}) collective-permute-start(bf16[128,462]{0,1:T(8,128)(2,1)S(1)} %collective-permute-done.25), channel_id=1, source_target_pairs={{0,32},{32,64},{64,96},{96,128},{128,160},{160,192},{192,224},{224... | collective-permute-start | bytes 354824 | tf_op jit(solution)/shard_map/ppermute | solution.py:48
  226.9 341.0 %collective-permute-start.28 = (bf16[128,462]{0,1:T(8,128)(2,1)}, bf16[128,462]{0,1:T(8,128)(2,1)}, u32[]{:S(2)}, u32[]{:S(2)}) collective-permute-start(bf16[128,462]{0,1:T(8,128)(2,1)} %collective-permute-done.26), channel_id=1, source_target_pairs={{0,480},{32,0},{64,32},{96,64},{128,96},{160,128},{192,160},{224,1... | collective-permute-start | bytes 354824 | tf_op jit(solution)/shard_map/ppermute | solution.py:51
  232.6 348.7 %collective-permute-start.29 = (bf16[128,462]{0,1:T(8,128)(2,1)}, bf16[128,462]{0,1:T(8,128)(2,1)}, u32[]{:S(2)}, u32[]{:S(2)}) collective-permute-start(bf16[128,462]{0,1:T(8,128)(2,1)} %collective-permute-done.27), channel_id=1, source_target_pairs={{0,32},{32,64},{64,96},{96,128},{128,160},{160,192},{192,224},{224... | collective-permute-start | bytes 354824 | tf_op jit(solution)/shard_map/ppermute | solution.py:48
  (34 other events, 1529.1 us)
Sparse Core Ops, SparseCore 0:
  11.1 63.0 all-gather.2
  86.3 57.4 all-gather.4
  597.6 103.6 reduce-scatter.1
where the time goes:
time: 721 us; the launch traced here: 708 us
  local copies, waits for them, and re-layouts  361 us (50%)
  starting transfers between devices  164 us (23%)
  waiting for transfers between devices  142 us (20%)
  matrix products  17.2 us (2%)
  between operations  15.8 us (2%)
  other arithmetic  7.71 us (1%)
    dynamic_update_slice x16, local copies, waits for them, and re-layouts, ring_all_gather(): out = lax.dynamic_update_index_in_dim(out, a, (me - s + n) % n, 0)  164 us
    dynamic_update_slice x14, local copies, waits for them, and re-layouts, ring_all_gather(): out = lax.dynamic_update_index_in_dim(out, b, (me + s) % n, 0)  143 us
    reduce_scatter x1, waiting for transfers between devices, shards(): lax.psum_scatter((contract_cols(gate_grad, w_gate) + contract_cols(up_gra...  93.5 us
    ppermute x14, starting transfers between devices, ring_all_gather(): b = lax.ppermute(b, axis, down)  76.6 us
    ppermute x7, starting transfers between devices, ring_reduce_scatter(): b = lax.ppermute(b.astype(wire_dtype), axis, down).astype(jnp.float32)  37.6 us
    all_gather x1, waiting for transfers between devices, shards(): all_grad_out = lax.all_gather(grad_out, 'col', axis=0, tiled=True)  36 us
    ppermute x16, starting transfers between devices, ring_all_gather(): a = lax.ppermute(a, axis, up)  32.8 us
    dynamic_update_slice x2, local copies, waits for them, and re-layouts, ring_all_gather(): out = lax.dynamic_update_index_in_dim(out, x, me, 0)  20.6 us
  transfers between devices with their start and end apart: 48, of which 13 were waited for; matrix products, arithmetic and copies ran while one was open for 54% of the time, Pallas kernels for 0%

commit v1 on v0

--- a/solution.py
+++ b/solution.py
@@ -81,7 +81,14 @@
     tokens_row, hidden_units = gate_pre.shape
     pre = jnp.stack([gate_pre, up_pre], axis=1)
     all_pre = ring_all_gather(pre, "row", n_row).reshape((n_row * tokens_row, 2, hidden_units))
-    all_grad_out = lax.all_gather(grad_out, "col", axis=0, tiled=True)
+
+    def scan_thing(payload):
+        z_new = lax.axis_size("col")
+        low = jnp.stack([payload] * z_new, axis=0)
+        t_next = lax.all_to_all(low, split_axis=0, concat_axis=0, axis_name="col")
+        return jnp.concatenate(t_next, axis=0)
+
+    all_grad_out = scan_thing(grad_out)
     all_inputs = lax.all_gather(inputs, "col", axis=0, tiled=True)
     part = contract_cols(all_grad_out, w_down).astype(jnp.bfloat16)
     part = part.reshape((n_row, tokens_row, hidden_units))

time: 721 us -> 695 us (0.964)
  waiting for transfers between devices: 142 us -> 103 us
  starting transfers between devices: 164 us -> 175 us
    all_gather x1 -> x0, waiting for transfers between devices: 36 us -> none  [shards(): all_grad_out = lax.all_gather(grad_out, 'col', axis=0, tiled=True)]
    all_to_all x0 -> x1, starting transfers between devices: none -> 9.68 us  [scan_thing(): t_next = lax.all_to_all(low, split_axis=0, concat_axis=0, axis_name='col')]
  transfers between devices with their start and end apart: 48 -> 48, of which waited for: 13 -> 14; matrix products, arithmetic and copies ran while one was open for 54% -> 56% of each run, Pallas kernels for 0% -> 0%
where the time goes in v1:
time: 695 us; the launch traced here: 682 us
  local copies, waits for them, and re-layouts  364 us (52%)
  starting transfers between devices  175 us (25%)
  waiting for transfers between devices  103 us (15%)
  matrix products  16.9 us (2%)
  between operations  16.2 us (2%)
    dynamic_update_slice x16, local copies, waits for them, and re-layouts, ring_all_gather(): out = lax.dynamic_update_index_in_dim(out, a, (me - s + n) % n, 0)  164 us
    dynamic_update_slice x14, local copies, waits for them, and re-layouts, ring_all_gather(): out = lax.dynamic_update_index_in_dim(out, b, (me + s) % n, 0)  143 us
    reduce_scatter x1, waiting for transfers between devices, shards(): lax.psum_scatter((contract_cols(gate_grad, w_gate) + contract_cols(up_gra...  88 us
    ppermute x14, starting transfers between devices, ring_all_gather(): b = lax.ppermute(b, axis, down)  81.8 us
    ppermute x7, starting transfers between devices, ring_reduce_scatter(): b = lax.ppermute(b.astype(wire_dtype), axis, down).astype(jnp.float32)  37.6 us
    ppermute x16, starting transfers between devices, ring_all_gather(): a = lax.ppermute(a, axis, up)  30.7 us
    dynamic_update_slice x2, local copies, waits for them, and re-layouts, ring_all_gather(): out = lax.dynamic_update_index_in_dim(out, x, me, 0)  20.6 us
    ppermute x8, starting transfers between devices, ring_reduce_scatter(): a = lax.ppermute(a.astype(wire_dtype), axis, up).astype(jnp.float32)  15.5 us
  transfers between devices with their start and end apart: 48, of which 14 were waited for; matrix products, arithmetic and copies ran while one was open for 56% of the time, Pallas kernels for 0%

profile of v1, /device:TPU:2, one launch (start us, length us, event | category | flops | bytes accessed | tf_op | source)
XLA Modules:
  0.0 681.6 jit_solution(9949438827543421143)
XLA Ops:
  9.6 9.7 %all-to-all-start = ((bf16[32,64,512]{2,1,0:T(8,128)(2,1)}), bf16[32,64,512]{2,1,0:T(8,128)(2,1)S(1)}, u32[]{:S(2)}, u32[]{:S(2)}) async-start(bf16[32,64,512]{2,1,0:T(8,128)(2,1)} %stack.8), calls=%async_computation | async-start | bytes 4194304 | tf_op jit(solution)/shard_map/all_to_all | solution.py:88
  21.3 9.5 %collective-permute-start.31 = (bf16[128,2,462]{0,2,1:T(8,128)(2,1)S(1)}, bf16[128,2,462]{0,2,1:T(8,128)(2,1)}, u32[]{:S(2)}, u32[]{:S(2)}) collective-permute-start(bf16[128,2,462]{0,2,1:T(8,128)(2,1)S(1)} %get-tuple-element.22), channel_id=1, source_target_pairs={{0,480},{32,0},{64,32},{96,64},{128,96},{160,128},{192,160},{224,1... | collective-permute-start | bytes 709640 | tf_op jit(solution)/shard_map/ppermute | solution.py:51
  37.1 5.1 collective-permute-start.33
  57.7 9.4 %collective-permute-start.35 = (bf16[128,2,462]{0,2,1:T(8,128)(2,1)}, bf16[128,2,462]{0,2,1:T(8,128)(2,1)S(1)}, u32[]{:S(2)}, u32[]{:S(2)}) collective-permute-start(bf16[128,2,462]{0,2,1:T(8,128)(2,1)} %collective-permute-done.33), channel_id=1, source_target_pairs={{0,480},{32,0},{64,32},{96,64},{128,96},{160,128},{192,160},{224,1... | collective-permute-start | bytes 709640 | tf_op jit(solution)/shard_map/ppermute | solution.py:51
  78.1 5.1 collective-permute-start.9
  87.2 5.1 collective-permute-start.10
  94.8 5.5 collective-permute-start.11
  102.7 5.5 collective-permute-start.12
  110.7 5.5 collective-permute-start.13
  119.2 5.6 collective-permute-start.14
  160.6 5.5 collective-permute-start.20
  183.3 5.6 collective-permute-start.24
  191.2 5.1 collective-permute-start.43
  198.3 5.1 collective-permute-start.26
  205.8 5.6 collective-permute-start.28
  216.5 14.4 %dynamic_update_slice.114 = bf16[16,128,2,462]{1,0,3,2:T(8,128)(2,1)} dynamic-update-slice(bf16[16,128,2,462]{1,0,3,2:T(8,128)(2,1)} %broadcast_in_dim.121, bf16[1,128,2,462]{1,0,3,2:T(2,128)(2,1)S(1)} %copy.56, s32[]{:T(128)S(6)} %select_n.304, s32[]{:T(128)} %constant.338.clone.1, s32[]{:T(128)} %constant.338.clone.1, s32[]{:T(128)} %constant.338.clone.1) | dynamic-update-slice | bytes 473092 | tf_op jit(solution)/shard_map/jit(dynamic_update_index_in_dim)/dynamic_update_slice | solution.py:44
  232.7 14.3 %dynamic_update_slice.115 = bf16[16,128,2,462]{1,0,3,2:T(8,128)(2,1)} dynamic-update-slice(bf16[16,128,2,462]{1,0,3,2:T(8,128)(2,1)} %dynamic_update_slice.114, bf16[1,128,2,462]{1,0,3,2:T(2,128)(2,1)S(1)} %copy.57, s32[]{:T(128)S(6)} %select_n.306, s32[]{:T(128)} %constant.338.clone.1, s32[]{:T(128)} %constant.338.clone.1, s32[]{:T(128)} %constant.338.clone.1) | dynamic-update-slice | bytes 473092 | tf_op jit(solution)/shard_map/jit(dynamic_update_index_in_dim)/dynamic_update_slice | solution.py:49
  246.9 14.3 %dynamic_update_slice.116 = bf16[16,128,2,462]{1,0,3,2:T(8,128)(2,1)} dynamic-update-slice(bf16[16,128,2,462]{1,0,3,2:T(8,128)(2,1)} %dynamic_update_slice.115, bf16[1,128,2,462]{1,0,3,2:T(2,128)(2,1)S(1)} %copy.58, s32[]{:T(128)S(6)} %select_n.308, s32[]{:T(128)} %constant.338.clone.1, s32[]{:T(128)} %constant.338.clone.1, s32[]{:T(128)} %constant.338.clone.1) | dynamic-update-slice | bytes 473092 | tf_op jit(solution)/shard_map/jit(dynamic_update_index_in_dim)/dynamic_update_slice | solution.py:52
  263.9 14.3 %dynamic_update_slice.117 = bf16[16,128,2,462]{1,0,3,2:T(8,128)(2,1)} dynamic-update-slice(bf16[16,128,2,462]{1,0,3,2:T(8,128)(2,1)} %dynamic_update_slice.116, bf16[1,128,2,462]{1,0,3,2:T(2,128)(2,1)S(1)} %copy.59, s32[]{:T(128)S(6)} %select_n.310, s32[]{:T(128)} %constant.338.clone.1, s32[]{:T(128)} %constant.338.clone.1, s32[]{:T(128)} %constant.338.clone.1) | dynamic-update-slice | bytes 473092 | tf_op jit(solution)/shard_map/jit(dynamic_update_index_in_dim)/dynamic_update_slice | solution.py:49
  278.2 14.3 %dynamic_update_slice.118 = bf16[16,128,2,462]{1,0,3,2:T(8,128)(2,1)} dynamic-update-slice(bf16[16,128,2,462]{1,0,3,2:T(8,128)(2,1)} %dynamic_update_slice.117, bf16[1,128,2,462]{1,0,3,2:T(2,128)(2,1)S(1)} %copy.60, s32[]{:T(128)S(6)} %select_n.312, s32[]{:T(128)} %constant.338.clone.1, s32[]{:T(128)} %constant.338.clone.1, s32[]{:T(128)} %constant.338.clone.1) | dynamic-update-slice | bytes 473092 | tf_op jit(solution)/shard_map/jit(dynamic_update_index_in_dim)/dynamic_update_slice | solution.py:52
  294.2 14.3 %dynamic_update_slice.119 = bf16[16,128,2,462]{1,0,3,2:T(8,128)(2,1)} dynamic-update-slice(bf16[16,128,2,462]{1,0,3,2:T(8,128)(2,1)} %dynamic_update_slice.118, bf16[1,128,2,462]{1,0,3,2:T(2,128)(2,1)S(1)} %copy.61, s32[]{:T(128)S(6)} %select_n.314, s32[]{:T(128)} %constant.338.clone.1, s32[]{:T(128)} %constant.338.clone.1, s32[]{:T(128)} %constant.338.clone.1) | dynamic-update-slice | bytes 473092 | tf_op jit(solution)/shard_map/jit(dynamic_update_index_in_dim)/dynamic_update_slice | solution.py:49
  308.5 14.3 %dynamic_update_slice.120 = bf16[16,128,2,462]{1,0,3,2:T(8,128)(2,1)} dynamic-update-slice(bf16[16,128,2,462]{1,0,3,2:T(8,128)(2,1)} %dynamic_update_slice.119, bf16[1,128,2,462]{1,0,3,2:T(2,128)(2,1)S(1)} %copy.62, s32[]{:T(128)S(6)} %select_n.316, s32[]{:T(128)} %constant.338.clone.1, s32[]{:T(128)} %constant.338.clone.1, s32[]{:T(128)} %constant.338.clone.1) | dynamic-update-slice | bytes 473092 | tf_op jit(solution)/shard_map/jit(dynamic_update_index_in_dim)/dynamic_update_slice | solution.py:52
  323.5 14.3 %dynamic_update_slice.121 = bf16[16,128,2,462]{1,0,3,2:T(8,128)(2,1)} dynamic-update-slice(bf16[16,128,2,462]{1,0,3,2:T(8,128)(2,1)} %dynamic_update_slice.120, bf16[1,128,2,462]{1,0,3,2:T(2,128)(2,1)S(1)} %copy.63, s32[]{:T(128)S(6)} %select_n.318, s32[]{:T(128)} %constant.338.clone.1, s32[]{:T(128)} %constant.338.clone.1, s32[]{:T(128)} %constant.338.clone.1) | dynamic-update-slice | bytes 473092 | tf_op jit(solution)/shard_map/jit(dynamic_update_index_in_dim)/dynamic_update_slice | solution.py:49
  337.8 14.3 %dynamic_update_slice.122 = bf16[16,128,2,462]{1,0,3,2:T(8,128)(2,1)} dynamic-update-slice(bf16[16,128,2,462]{1,0,3,2:T(8,128)(2,1)} %dynamic_update_slice.121, bf16[1,128,2,462]{1,0,3,2:T(2,128)(2,1)S(1)} %copy.64, s32[]{:T(128)S(6)} %select_n.320, s32[]{:T(128)} %constant.338.clone.1, s32[]{:T(128)} %constant.338.clone.1, s32[]{:T(128)} %constant.338.clone.1) | dynamic-update-slice | bytes 473092 | tf_op jit(solution)/shard_map/jit(dynamic_update_index_in_dim)/dynamic_update_slice | solution.py:52
  352.9 14.3 %dynamic_update_slice.123 = bf16[16,128,2,462]{1,0,3,2:T(8,128)(2,1)} dynamic-update-slice(bf16[16,128,2,462]{1,0,3,2:T(8,128)(2,1)} %dynamic_update_slice.122, bf16[1,128,2,462]{1,0,3,2:T(2,128)(2,1)S(1)} %copy.65, s32[]{:T(128)S(6)} %select_n.322, s32[]{:T(128)} %constant.338.clone.1, s32[]{:T(128)} %constant.338.clone.1, s32[]{:T(128)} %constant.338.clone.1) | dynamic-update-slice | bytes 473092 | tf_op jit(solution)/shard_map/jit(dynamic_update_index_in_dim)/dynamic_update_slice | solution.py:49
  367.2 14.3 %dynamic_update_slice.124 = bf16[16,128,2,462]{1,0,3,2:T(8,128)(2,1)} dynamic-update-slice(bf16[16,128,2,462]{1,0,3,2:T(8,128)(2,1)} %dynamic_update_slice.123, bf16[1,128,2,462]{1,0,3,2:T(2,128)(2,1)S(1)} %copy.66, s32[]{:T(128)S(6)} %select_n.324, s32[]{:T(128)} %constant.338.clone.1, s32[]{:T(128)} %constant.338.clone.1, s32[]{:T(128)} %constant.338.clone.1) | dynamic-update-slice | bytes 473092 | tf_op jit(solution)/shard_map/jit(dynamic_update_index_in_dim)/dynamic_update_slice | solution.py:52
  382.2 14.5 %dynamic_update_slice.125 = bf16[16,128,2,462]{1,0,3,2:T(8,128)(2,1)} dynamic-update-slice(bf16[16,128,2,462]{1,0,3,2:T(8,128)(2,1)} %dynamic_update_slice.124, bf16[1,128,2,462]{1,0,3,2:T(2,128)(2,1)S(1)} %copy.67, s32[]{:T(128)S(6)} %select_n.326, s32[]{:T(128)} %constant.338.clone.1, s32[]{:T(128)} %constant.338.clone.1, s32[]{:T(128)} %constant.338.clone.1) | dynamic-update-slice | bytes 473092 | tf_op jit(solution)/shard_map/jit(dynamic_update_index_in_dim)/dynamic_update_slice | solution.py:49
  396.7 14.3 %dynamic_update_slice.126 = bf16[16,128,2,462]{1,0,3,2:T(8,128)(2,1)} dynamic-update-slice(bf16[16,128,2,462]{1,0,3,2:T(8,128)(2,1)} %dynamic_update_slice.125, bf16[1,128,2,462]{1,0,3,2:T(2,128)(2,1)S(1)} %copy.68, s32[]{:T(128)S(6)} %select_n.328, s32[]{:T(128)} %constant.338.clone.1, s32[]{:T(128)} %constant.338.clone.1, s32[]{:T(128)} %constant.338.clone.1) | dynamic-update-slice | bytes 473092 | tf_op jit(solution)/shard_map/jit(dynamic_update_index_in_dim)/dynamic_update_slice | solution.py:52
  412.7 14.3 %dynamic_update_slice.127 = bf16[16,128,2,462]{1,0,3,2:T(8,128)(2,1)} dynamic-update-slice(bf16[16,128,2,462]{1,0,3,2:T(8,128)(2,1)} %dynamic_update_slice.126, bf16[1,128,2,462]{1,0,3,2:T(2,128)(2,1)S(1)} %copy.69, s32[]{:T(128)S(6)} %select_n.330, s32[]{:T(128)} %constant.338.clone.1, s32[]{:T(128)} %constant.338.clone.1, s32[]{:T(128)} %constant.338.clone.1) | dynamic-update-slice | bytes 473092 | tf_op jit(solution)/shard_map/jit(dynamic_update_index_in_dim)/dynamic_update_slice | solution.py:49
  427.0 14.3 %dynamic_update_slice.128 = bf16[16,128,2,462]{1,0,3,2:T(8,128)(2,1)} dynamic-update-slice(bf16[16,128,2,462]{1,0,3,2:T(8,128)(2,1)} %dynamic_update_slice.127, bf16[1,128,2,462]{1,0,3,2:T(2,128)(2,1)S(1)} %copy.70, s32[]{:T(128)S(6)} %select_n.332, s32[]{:T(128)} %constant.338.clone.1, s32[]{:T(128)} %constant.338.clone.1, s32[]{:T(128)} %constant.338.clone.1) | dynamic-update-slice | bytes 473092 | tf_op jit(solution)/shard_map/jit(dynamic_update_index_in_dim)/dynamic_update_slice | solution.py:52
  442.5 14.3 %dynamic_update_slice.129 = bf16[16,128,2,462]{1,0,3,2:T(8,128)(2,1)} dynamic-update-slice(bf16[16,128,2,462]{1,0,3,2:T(8,128)(2,1)} %dynamic_update_slice.128, bf16[1,128,2,462]{1,0,3,2:T(2,128)(2,1)S(1)} %copy.71, s32[]{:T(128)S(6)} %select_n.334, s32[]{:T(128)} %constant.338.clone.1, s32[]{:T(128)} %constant.338.clone.1, s32[]{:T(128)} %constant.338.clone.1) | dynamic-update-slice | bytes 473092 | tf_op jit(solution)/shard_map/jit(dynamic_update_index_in_dim)/dynamic_update_slice | solution.py:49
  461.8 6.2 dynamic_update_slice.98
  468.4 6.2 dynamic_update_slice.99
  474.6 6.2 dynamic_update_slice.100
  481.1 6.2 dynamic_update_slice.101
  487.3 6.2 dynamic_update_slice.102
  493.9 6.2 dynamic_update_slice.103
  500.0 6.2 dynamic_update_slice.104
  506.6 6.6 dynamic_update_slice.105
  513.1 6.2 dynamic_update_slice.106
  519.7 6.2 dynamic_update_slice.107
  525.9 6.2 dynamic_update_slice.108
  533.3 6.2 dynamic_update_slice.109
  539.5 6.2 dynamic_update_slice.110
  547.8 6.2 dynamic_update_slice.111
  554.0 6.2 dynamic_update_slice.112
  561.2 6.2 dynamic_update_slice.113
  586.7 88.0 %reduce-scatter.2.cloned.1.call-done = bf16[64,512]{1,0:T(8,128)(2,1)} async-done(((bf16[2048,512]{1,0:T(8,128)(2,1)}), bf16[64,512]{1,0:T(8,128)(2,1)}) %reduce-scatter.2.cloned.1.call-update) | async-done | bytes 65552 | tf_op jit(solution)/shard_map/reduce_scatter | solution.py:103
  (224 shorter events, 156.5 us)
Async XLA Ops:
  9.6 37.7 %all-to-all-start = ((bf16[32,64,512]{2,1,0:T(8,128)(2,1)}), bf16[32,64,512]{2,1,0:T(8,128)(2,1)S(1)}, u32[]{:S(2)}, u32[]{:S(2)}) async-start(bf16[32,64,512]{2,1,0:T(8,128)(2,1)} %stack.8), calls=%async_computation | async-start | bytes 4194304 | tf_op jit(solution)/shard_map/all_to_all | solution.py:88
  19.3 561.8 %all-gather.2.cloned.1.call-start = ((), (), s32[]{:S(2)}) async-start(), calls=%async_computation.3 | async-start | bytes 2162688 | tf_op jit(solution)/shard_map/all_gather | solution.py:92
  19.4 15.5 %collective-permute-start.30 = (bf16[128,2,462]{0,2,1:T(8,128)(2,1)S(1)}, bf16[128,2,462]{0,2,1:T(8,128)(2,1)S(1)}, u32[]{:S(2)}, u32[]{:S(2)}) collective-permute-start(bf16[128,2,462]{0,2,1:T(8,128)(2,1)S(1)} %get-tuple-element.22), channel_id=1, source_target_pairs={{0,32},{32,64},{64,96},{96,128},{128,160},{160,192},{192,224},{224... | collective-permute-start | bytes 709640 | tf_op jit(solution)/shard_map/ppermute | solution.py:48
  21.3 15.7 %collective-permute-start.31 = (bf16[128,2,462]{0,2,1:T(8,128)(2,1)S(1)}, bf16[128,2,462]{0,2,1:T(8,128)(2,1)}, u32[]{:S(2)}, u32[]{:S(2)}) collective-permute-start(bf16[128,2,462]{0,2,1:T(8,128)(2,1)S(1)} %get-tuple-element.22), channel_id=1, source_target_pairs={{0,480},{32,0},{64,32},{96,64},{128,96},{160,128},{192,160},{224,1... | collective-permute-start | bytes 709640 | tf_op jit(solution)/shard_map/ppermute | solution.py:51
  34.9 10.4 %collective-permute-start.32 = (bf16[128,2,462]{0,2,1:T(8,128)(2,1)S(1)}, bf16[128,2,462]{0,2,1:T(8,128)(2,1)}, u32[]{:S(2)}, u32[]{:S(2)}) collective-permute-start(bf16[128,2,462]{0,2,1:T(8,128)(2,1)S(1)} %collective-permute-done.30), channel_id=1, source_target_pairs={{0,32},{32,64},{64,96},{96,128},{128,160},{160,192},{192,224},{224... | collective-permute-start | bytes 709640 | tf_op jit(solution)/shard_map/ppermute | solution.py:48
  37.1 20.6 %collective-permute-start.33 = (bf16[128,2,462]{0,2,1:T(8,128)(2,1)}, bf16[128,2,462]{0,2,1:T(8,128)(2,1)}, u32[]{:S(2)}, u32[]{:S(2)}) collective-permute-start(bf16[128,2,462]{0,2,1:T(8,128)(2,1)} %collective-permute-done.31), channel_id=1, source_target_pairs={{0,480},{32,0},{64,32},{96,64},{128,96},{160,128},{192,160},{224,1... | collective-permute-start | bytes 709640 | tf_op jit(solution)/shard_map/ppermute | solution.py:51
  45.4 21.7 %collective-permute-start.34 = (bf16[128,2,462]{0,2,1:T(8,128)(2,1)}, bf16[128,2,462]{0,2,1:T(8,128)(2,1)}, u32[]{:S(2)}, u32[]{:S(2)}) collective-permute-start(bf16[128,2,462]{0,2,1:T(8,128)(2,1)} %collective-permute-done.32), channel_id=1, source_target_pairs={{0,32},{32,64},{64,96},{96,128},{128,160},{160,192},{192,224},{224... | collective-permute-start | bytes 709640 | tf_op jit(solution)/shard_map/ppermute | solution.py:48
  55.6 18.6 %collective-permute-start = (bf16[128,462]{0,1:T(8,128)(2,1)S(1)}, bf16[128,462]{0,1:T(8,128)(2,1)}, u32[]{:S(2)}, u32[]{:S(2)}) collective-permute-start(bf16[128,462]{0,1:T(8,128)(2,1)S(1)} %bitcast.211), channel_id=1, source_target_pairs={{0,32},{32,64},{64,96},{96,128},{128,160},{160,192},{192,224},{224... | collective-permute-start | bytes 354824 | tf_op jit(solution)/shard_map/ppermute | solution.py:70
  57.6 617.0 %reduce-scatter.2.cloned.1.call-start = ((), (), s32[]{:S(2)}) async-start(), calls=%async_computation.2 | async-start | bytes 2162688 | tf_op jit(solution)/shard_map/reduce_scatter | solution.py:103
  57.7 69.4 %collective-permute-start.35 = (bf16[128,2,462]{0,2,1:T(8,128)(2,1)}, bf16[128,2,462]{0,2,1:T(8,128)(2,1)S(1)}, u32[]{:S(2)}, u32[]{:S(2)}) collective-permute-start(bf16[128,2,462]{0,2,1:T(8,128)(2,1)} %collective-permute-done.33), channel_id=1, source_target_pairs={{0,480},{32,0},{64,32},{96,64},{128,96},{160,128},{192,160},{224,1... | collective-permute-start | bytes 709640 | tf_op jit(solution)/shard_map/ppermute | solution.py:51
  67.1 65.2 %collective-permute-start.36 = (bf16[128,2,462]{0,2,1:T(8,128)(2,1)}, bf16[128,2,462]{0,2,1:T(8,128)(2,1)S(1)}, u32[]{:S(2)}, u32[]{:S(2)}) collective-permute-start(bf16[128,2,462]{0,2,1:T(8,128)(2,1)} %collective-permute-done.34), channel_id=1, source_target_pairs={{0,32},{32,64},{64,96},{96,128},{128,160},{160,192},{192,224},{224... | collective-permute-start | bytes 709640 | tf_op jit(solution)/shard_map/ppermute | solution.py:48
  69.0 8.1 %collective-permute-start.8 = (bf16[128,462]{0,1:T(8,128)(2,1)S(1)}, bf16[128,462]{0,1:T(8,128)(2,1)S(1)}, u32[]{:S(2)}, u32[]{:S(2)}) collective-permute-start(bf16[128,462]{0,1:T(8,128)(2,1)S(1)} %bitcast.212), channel_id=1, source_target_pairs={{0,480},{32,0},{64,32},{96,64},{128,96},{160,128},{192,160},{224,1... | collective-permute-start | bytes 354824 | tf_op jit(solution)/shard_map/ppermute | solution.py:74
  75.2 8.1 %collective-permute-start.1 = (bf16[128,462]{0,1:T(8,128)(2,1)S(1)}, bf16[128,462]{0,1:T(8,128)(2,1)S(1)}, u32[]{:S(2)}, u32[]{:S(2)}) collective-permute-start(bf16[128,462]{0,1:T(8,128)(2,1)S(1)} %fusion.39), channel_id=1, source_target_pairs={{0,32},{32,64},{64,96},{96,128},{128,160},{160,192},{192,224},{224... | collective-permute-start | bytes 354824 | tf_op jit(solution)/shard_map/ppermute | solution.py:70
  78.1 8.1 %collective-permute-start.9 = (bf16[128,462]{0,1:T(8,128)(2,1)S(1)}, bf16[128,462]{0,1:T(8,128)(2,1)S(1)}, u32[]{:S(2)}, u32[]{:S(2)}) collective-permute-start(bf16[128,462]{0,1:T(8,128)(2,1)S(1)} %fusion.32), channel_id=1, source_target_pairs={{0,480},{32,0},{64,32},{96,64},{128,96},{160,128},{192,160},{224,1... | collective-permute-start | bytes 354824 | tf_op jit(solution)/shard_map/ppermute | solution.py:74
  84.3 8.1 %collective-permute-start.2 = (bf16[128,462]{0,1:T(8,128)(2,1)S(1)}, bf16[128,462]{0,1:T(8,128)(2,1)S(1)}, u32[]{:S(2)}, u32[]{:S(2)}) collective-permute-start(bf16[128,462]{0,1:T(8,128)(2,1)S(1)} %fusion.38), channel_id=1, source_target_pairs={{0,32},{32,64},{64,96},{96,128},{128,160},{160,192},{192,224},{224... | collective-permute-start | bytes 354824 | tf_op jit(solution)/shard_map/ppermute | solution.py:70
  87.2 7.5 %collective-permute-start.10 = (bf16[128,462]{0,1:T(8,128)(2,1)S(1)}, bf16[128,462]{0,1:T(8,128)(2,1)S(1)}, u32[]{:S(2)}, u32[]{:S(2)}) collective-permute-start(bf16[128,462]{0,1:T(8,128)(2,1)S(1)} %fusion.31), channel_id=1, source_target_pairs={{0,480},{32,0},{64,32},{96,64},{128,96},{160,128},{192,160},{224,1... | collective-permute-start | bytes 354824 | tf_op jit(solution)/shard_map/ppermute | solution.py:74
  92.4 7.9 %collective-permute-start.3 = (bf16[128,462]{0,1:T(8,128)(2,1)S(1)}, bf16[128,462]{0,1:T(8,128)(2,1)S(1)}, u32[]{:S(2)}, u32[]{:S(2)}) collective-permute-start(bf16[128,462]{0,1:T(8,128)(2,1)S(1)} %fusion.37), channel_id=1, source_target_pairs={{0,32},{32,64},{64,96},{96,128},{128,160},{160,192},{192,224},{224... | collective-permute-start | bytes 354824 | tf_op jit(solution)/shard_map/ppermute | solution.py:70
  94.8 7.9 %collective-permute-start.11 = (bf16[128,462]{0,1:T(8,128)(2,1)S(1)}, bf16[128,462]{0,1:T(8,128)(2,1)S(1)}, u32[]{:S(2)}, u32[]{:S(2)}) collective-permute-start(bf16[128,462]{0,1:T(8,128)(2,1)S(1)} %fusion.30), channel_id=1, source_target_pairs={{0,480},{32,0},{64,32},{96,64},{128,96},{160,128},{192,160},{224,1... | collective-permute-start | bytes 354824 | tf_op jit(solution)/shard_map/ppermute | solution.py:74
  100.4 7.9 %collective-permute-start.4 = (bf16[128,462]{0,1:T(8,128)(2,1)S(1)}, bf16[128,462]{0,1:T(8,128)(2,1)S(1)}, u32[]{:S(2)}, u32[]{:S(2)}) collective-permute-start(bf16[128,462]{0,1:T(8,128)(2,1)S(1)} %fusion.36), channel_id=1, source_target_pairs={{0,32},{32,64},{64,96},{96,128},{128,160},{160,192},{192,224},{224... | collective-permute-start | bytes 354824 | tf_op jit(solution)/shard_map/ppermute | solution.py:70
  102.7 7.9 %collective-permute-start.12 = (bf16[128,462]{0,1:T(8,128)(2,1)S(1)}, bf16[128,462]{0,1:T(8,128)(2,1)S(1)}, u32[]{:S(2)}, u32[]{:S(2)}) collective-permute-start(bf16[128,462]{0,1:T(8,128)(2,1)S(1)} %fusion.29), channel_id=1, source_target_pairs={{0,480},{32,0},{64,32},{96,64},{128,96},{160,128},{192,160},{224,1... | collective-permute-start | bytes 354824 | tf_op jit(solution)/shard_map/ppermute | solution.py:74
  108.3 7.9 %collective-permute-start.5 = (bf16[128,462]{0,1:T(8,128)(2,1)S(1)}, bf16[128,462]{0,1:T(8,128)(2,1)S(1)}, u32[]{:S(2)}, u32[]{:S(2)}) collective-permute-start(bf16[128,462]{0,1:T(8,128)(2,1)S(1)} %fusion.35), channel_id=1, source_target_pairs={{0,32},{32,64},{64,96},{96,128},{128,160},{160,192},{192,224},{224... | collective-permute-start | bytes 354824 | tf_op jit(solution)/shard_map/ppermute | solution.py:70
  110.7 8.5 %collective-permute-start.13 = (bf16[128,462]{0,1:T(8,128)(2,1)S(1)}, bf16[128,462]{0,1:T(8,128)(2,1)S(1)}, u32[]{:S(2)}, u32[]{:S(2)}) collective-permute-start(bf16[128,462]{0,1:T(8,128)(2,1)S(1)} %fusion.28), channel_id=1, source_target_pairs={{0,480},{32,0},{64,32},{96,64},{128,96},{160,128},{192,160},{224,1... | collective-permute-start | bytes 354824 | tf_op jit(solution)/shard_map/ppermute | solution.py:74
  116.3 8.9 %collective-permute-start.6 = (bf16[128,462]{0,1:T(8,128)(2,1)S(1)}, bf16[128,462]{0,1:T(8,128)(2,1)S(1)}, u32[]{:S(2)}, u32[]{:S(2)}) collective-permute-start(bf16[128,462]{0,1:T(8,128)(2,1)S(1)} %fusion.34), channel_id=1, source_target_pairs={{0,32},{32,64},{64,96},{96,128},{128,160},{160,192},{192,224},{224... | collective-permute-start | bytes 354824 | tf_op jit(solution)/shard_map/ppermute | solution.py:70
  119.2 15.0 %collective-permute-start.14 = (bf16[128,462]{0,1:T(8,128)(2,1)S(1)}, bf16[128,462]{0,1:T(8,128)(2,1)S(1)}, u32[]{:S(2)}, u32[]{:S(2)}) collective-permute-start(bf16[128,462]{0,1:T(8,128)(2,1)S(1)} %fusion.27), channel_id=1, source_target_pairs={{0,480},{32,0},{64,32},{96,64},{128,96},{160,128},{192,160},{224,1... | collective-permute-start | bytes 354824 | tf_op jit(solution)/shard_map/ppermute | solution.py:74
  125.2 9.2 %collective-permute-start.7 = (bf16[128,462]{0,1:T(8,128)(2,1)S(1)}, bf16[128,462]{0,1:T(8,128)(2,1)S(1)}, u32[]{:S(2)}, u32[]{:S(2)}) collective-permute-start(bf16[128,462]{0,1:T(8,128)(2,1)S(1)} %fusion.33), channel_id=1, source_target_pairs={{0,32},{32,64},{64,96},{96,128},{128,160},{160,192},{192,224},{224... | collective-permute-start | bytes 354824 | tf_op jit(solution)/shard_map/ppermute | solution.py:70
  127.2 18.8 %collective-permute-start.37 = (bf16[128,2,462]{0,2,1:T(8,128)(2,1)S(1)}, bf16[128,2,462]{0,2,1:T(8,128)(2,1)S(1)}, u32[]{:S(2)}, u32[]{:S(2)}) collective-permute-start(bf16[128,2,462]{0,2,1:T(8,128)(2,1)S(1)} %collective-permute-done.35), channel_id=1, source_target_pairs={{0,480},{32,0},{64,32},{96,64},{128,96},{160,128},{192,160},{224,1... | collective-permute-start | bytes 709640 | tf_op jit(solution)/shard_map/ppermute | solution.py:51
  132.3 18.8 %collective-permute-start.38 = (bf16[128,2,462]{0,2,1:T(8,128)(2,1)S(1)}, bf16[128,2,462]{0,2,1:T(8,128)(2,1)S(1)}, u32[]{:S(2)}, u32[]{:S(2)}) collective-permute-start(bf16[128,2,462]{0,2,1:T(8,128)(2,1)S(1)} %collective-permute-done.36), channel_id=1, source_target_pairs={{0,32},{32,64},{64,96},{96,128},{128,160},{160,192},{192,224},{224... | collective-permute-start | bytes 709640 | tf_op jit(solution)/shard_map/ppermute | solution.py:48
  134.5 9.6 %collective-permute-start.15 = (bf16[128,462]{0,1:T(8,128)(2,1)S(1)}, bf16[128,462]{0,1:T(8,128)(2,1)S(1)}, u32[]{:S(2)}, u32[]{:S(2)}) collective-permute-start(bf16[128,462]{0,1:T(8,128)(2,1)S(1)} %fusion.41), channel_id=1, source_target_pairs={{0,32},{32,64},{64,96},{96,128},{128,160},{160,192},{192,224},{224... | collective-permute-start | bytes 354824 | tf_op jit(solution)/shard_map/ppermute | solution.py:48
  136.4 16.7 %collective-permute-start.16 = (bf16[128,462]{0,1:T(8,128)(2,1)S(1)}, bf16[128,462]{0,1:T(8,128)(2,1)S(1)}, u32[]{:S(2)}, u32[]{:S(2)}) collective-permute-start(bf16[128,462]{0,1:T(8,128)(2,1)S(1)} %fusion.41), channel_id=1, source_target_pairs={{0,480},{32,0},{64,32},{96,64},{128,96},{160,128},{192,160},{224,1... | collective-permute-start | bytes 354824 | tf_op jit(solution)/shard_map/ppermute | solution.py:51
  144.1 14.2 %collective-permute-start.17 = (bf16[128,462]{0,1:T(8,128)(2,1)S(1)}, bf16[128,462]{0,1:T(8,128)(2,1)S(1)}, u32[]{:S(2)}, u32[]{:S(2)}) collective-permute-start(bf16[128,462]{0,1:T(8,128)(2,1)S(1)} %collective-permute-done.15), channel_id=1, source_target_pairs={{0,32},{32,64},{64,96},{96,128},{128,160},{160,192},{192,224},{224... | collective-permute-start | bytes 354824 | tf_op jit(solution)/shard_map/ppermute | solution.py:48
  146.0 22.1 %collective-permute-start.39 = (bf16[128,2,462]{0,2,1:T(8,128)(2,1)S(1)}, bf16[128,2,462]{0,2,1:T(8,128)(2,1)S(1)}, u32[]{:S(2)}, u32[]{:S(2)}) collective-permute-start(bf16[128,2,462]{0,2,1:T(8,128)(2,1)S(1)} %collective-permute-done.37), channel_id=1, source_target_pairs={{0,480},{32,0},{64,32},{96,64},{128,96},{160,128},{192,160},{224,1... | collective-permute-start | bytes 709640 | tf_op jit(solution)/shard_map/ppermute | solution.py:51
  151.2 22.1 %collective-permute-start.40 = (bf16[128,2,462]{0,2,1:T(8,128)(2,1)S(1)}, bf16[128,2,462]{0,2,1:T(8,128)(2,1)S(1)}, u32[]{:S(2)}, u32[]{:S(2)}) collective-permute-start(bf16[128,2,462]{0,2,1:T(8,128)(2,1)S(1)} %collective-permute-done.38), channel_id=1, source_target_pairs={{0,32},{32,64},{64,96},{96,128},{128,160},{160,192},{192,224},{224... | collective-permute-start | bytes 709640 | tf_op jit(solution)/shard_map/ppermute | solution.py:48
  153.1 7.5 %collective-permute-start.18 = (bf16[128,462]{0,1:T(8,128)(2,1)S(1)}, bf16[128,462]{0,1:T(8,128)(2,1)S(1)}, u32[]{:S(2)}, u32[]{:S(2)}) collective-permute-start(bf16[128,462]{0,1:T(8,128)(2,1)S(1)} %collective-permute-done.16), channel_id=1, source_target_pairs={{0,480},{32,0},{64,32},{96,64},{128,96},{160,128},{192,160},{224,1... | collective-permute-start | bytes 354824 | tf_op jit(solution)/shard_map/ppermute | solution.py:51
  158.3 7.9 %collective-permute-start.19 = (bf16[128,462]{0,1:T(8,128)(2,1)S(1)}, bf16[128,462]{0,1:T(8,128)(2,1)S(1)}, u32[]{:S(2)}, u32[]{:S(2)}) collective-permute-start(bf16[128,462]{0,1:T(8,128)(2,1)S(1)} %collective-permute-done.17), channel_id=1, source_target_pairs={{0,32},{32,64},{64,96},{96,128},{128,160},{160,192},{192,224},{224... | collective-permute-start | bytes 354824 | tf_op jit(solution)/shard_map/ppermute | solution.py:48
  160.6 14.6 %collective-permute-start.20 = (bf16[128,462]{0,1:T(8,128)(2,1)S(1)}, bf16[128,462]{0,1:T(8,128)(2,1)S(1)}, u32[]{:S(2)}, u32[]{:S(2)}) collective-permute-start(bf16[128,462]{0,1:T(8,128)(2,1)S(1)} %collective-permute-done.18), channel_id=1, source_target_pairs={{0,480},{32,0},{64,32},{96,64},{128,96},{160,128},{192,160},{224,1... | collective-permute-start | bytes 354824 | tf_op jit(solution)/shard_map/ppermute | solution.py:51
  166.2 14.2 %collective-permute-start.21 = (bf16[128,462]{0,1:T(8,128)(2,1)S(1)}, bf16[128,462]{0,1:T(8,128)(2,1)S(1)}, u32[]{:S(2)}, u32[]{:S(2)}) collective-permute-start(bf16[128,462]{0,1:T(8,128)(2,1)S(1)} %collective-permute-done.19), channel_id=1, source_target_pairs={{0,32},{32,64},{64,96},{96,128},{128,160},{160,192},{192,224},{224... | collective-permute-start | bytes 354824 | tf_op jit(solution)/shard_map/ppermute | solution.py:48
  168.2 23.0 %collective-permute-start.41 = (bf16[128,2,462]{0,2,1:T(8,128)(2,1)S(1)}, bf16[128,2,462]{0,2,1:T(8,128)(2,1)S(1)}, u32[]{:S(2)}, u32[]{:S(2)}) collective-permute-start(bf16[128,2,462]{0,2,1:T(8,128)(2,1)S(1)} %collective-permute-done.39), channel_id=1, source_target_pairs={{0,480},{32,0},{64,32},{96,64},{128,96},{160,128},{192,160},{224,1... | collective-permute-start | bytes 709640 | tf_op jit(solution)/shard_map/ppermute | solution.py:51
  173.3 23.0 %collective-permute-start.42 = (bf16[128,2,462]{0,2,1:T(8,128)(2,1)S(1)}, bf16[128,2,462]{0,2,1:T(8,128)(2,1)S(1)}, u32[]{:S(2)}, u32[]{:S(2)}) collective-permute-start(bf16[128,2,462]{0,2,1:T(8,128)(2,1)S(1)} %collective-permute-done.40), channel_id=1, source_target_pairs={{0,32},{32,64},{64,96},{96,128},{128,160},{160,192},{192,224},{224... | collective-permute-start | bytes 709640 | tf_op jit(solution)/shard_map/ppermute | solution.py:48
  175.3 8.1 %collective-permute-start.22 = (bf16[128,462]{0,1:T(8,128)(2,1)S(1)}, bf16[128,462]{0,1:T(8,128)(2,1)S(1)}, u32[]{:S(2)}, u32[]{:S(2)}) collective-permute-start(bf16[128,462]{0,1:T(8,128)(2,1)S(1)} %collective-permute-done.20), channel_id=1, source_target_pairs={{0,480},{32,0},{64,32},{96,64},{128,96},{160,128},{192,160},{224,1... | collective-permute-start | bytes 354824 | tf_op jit(solution)/shard_map/ppermute | solution.py:51
  180.4 8.8 %collective-permute-start.23 = (bf16[128,462]{0,1:T(8,128)(2,1)S(1)}, bf16[128,462]{0,1:T(8,128)(2,1)S(1)}, u32[]{:S(2)}, u32[]{:S(2)}) collective-permute-start(bf16[128,462]{0,1:T(8,128)(2,1)S(1)} %collective-permute-done.21), channel_id=1, source_target_pairs={{0,32},{32,64},{64,96},{96,128},{128,160},{160,192},{192,224},{224... | collective-permute-start | bytes 354824 | tf_op jit(solution)/shard_map/ppermute | solution.py:48
  183.3 14.9 %collective-permute-start.24 = (bf16[128,462]{0,1:T(8,128)(2,1)S(1)}, bf16[128,462]{0,1:T(8,128)(2,1)S(1)}, u32[]{:S(2)}, u32[]{:S(2)}) collective-permute-start(bf16[128,462]{0,1:T(8,128)(2,1)S(1)} %collective-permute-done.22), channel_id=1, source_target_pairs={{0,480},{32,0},{64,32},{96,64},{128,96},{160,128},{192,160},{224,1... | collective-permute-start | bytes 354824 | tf_op jit(solution)/shard_map/ppermute | solution.py:51
  189.2 14.2 %collective-permute-start.25 = (bf16[128,462]{0,1:T(8,128)(2,1)S(1)}, bf16[128,462]{0,1:T(8,128)(2,1)S(1)}, u32[]{:S(2)}, u32[]{:S(2)}) collective-permute-start(bf16[128,462]{0,1:T(8,128)(2,1)S(1)} %collective-permute-done.23), channel_id=1, source_target_pairs={{0,32},{32,64},{64,96},{96,128},{128,160},{160,192},{192,224},{224... | collective-permute-start | bytes 354824 | tf_op jit(solution)/shard_map/ppermute | solution.py:48
  191.2 220.2 %collective-permute-start.43 = (bf16[128,2,462]{0,2,1:T(8,128)(2,1)S(1)}, bf16[128,2,462]{0,2,1:T(8,128)(2,1)}, u32[]{:S(2)}, u32[]{:S(2)}) collective-permute-start(bf16[128,2,462]{0,2,1:T(8,128)(2,1)S(1)} %collective-permute-done.41), channel_id=1, source_target_pairs={{0,480},{32,0},{64,32},{96,64},{128,96},{160,128},{192,160},{224,1... | collective-permute-start | bytes 709640 | tf_op jit(solution)/shard_map/ppermute | solution.py:51
  196.3 244.9 %collective-permute-start.44 = (bf16[128,2,462]{0,2,1:T(8,128)(2,1)S(1)}, bf16[128,2,462]{0,2,1:T(8,128)(2,1)}, u32[]{:S(2)}, u32[]{:S(2)}) collective-permute-start(bf16[128,2,462]{0,2,1:T(8,128)(2,1)S(1)} %collective-permute-done.42), channel_id=1, source_target_pairs={{0,32},{32,64},{64,96},{96,128},{128,160},{160,192},{192,224},{224... | collective-permute-start | bytes 709640 | tf_op jit(solution)/shard_map/ppermute | solution.py:48
  198.3 7.5 %collective-permute-start.26 = (bf16[128,462]{0,1:T(8,128)(2,1)S(1)}, bf16[128,462]{0,1:T(8,128)(2,1)}, u32[]{:S(2)}, u32[]{:S(2)}) collective-permute-start(bf16[128,462]{0,1:T(8,128)(2,1)S(1)} %collective-permute-done.24), channel_id=1, source_target_pairs={{0,480},{32,0},{64,32},{96,64},{128,96},{160,128},{192,160},{224,1... | collective-permute-start | bytes 354824 | tf_op jit(solution)/shard_map/ppermute | solution.py:51
  203.5 8.0 %collective-permute-start.27 = (bf16[128,462]{0,1:T(8,128)(2,1)S(1)}, bf16[128,462]{0,1:T(8,128)(2,1)}, u32[]{:S(2)}, u32[]{:S(2)}) collective-permute-start(bf16[128,462]{0,1:T(8,128)(2,1)S(1)} %collective-permute-done.25), channel_id=1, source_target_pairs={{0,32},{32,64},{64,96},{96,128},{128,160},{160,192},{192,224},{224... | collective-permute-start | bytes 354824 | tf_op jit(solution)/shard_map/ppermute | solution.py:48
  205.8 340.9 %collective-permute-start.28 = (bf16[128,462]{0,1:T(8,128)(2,1)}, bf16[128,462]{0,1:T(8,128)(2,1)}, u32[]{:S(2)}, u32[]{:S(2)}) collective-permute-start(bf16[128,462]{0,1:T(8,128)(2,1)} %collective-permute-done.26), channel_id=1, source_target_pairs={{0,480},{32,0},{64,32},{96,64},{128,96},{160,128},{192,160},{224,1... | collective-permute-start | bytes 354824 | tf_op jit(solution)/shard_map/ppermute | solution.py:51
  211.5 348.6 %collective-permute-start.29 = (bf16[128,462]{0,1:T(8,128)(2,1)}, bf16[128,462]{0,1:T(8,128)(2,1)}, u32[]{:S(2)}, u32[]{:S(2)}) collective-permute-start(bf16[128,462]{0,1:T(8,128)(2,1)} %collective-permute-done.27), channel_id=1, source_target_pairs={{0,32},{32,64},{64,96},{96,128},{128,160},{160,192},{192,224},{224... | collective-permute-start | bytes 354824 | tf_op jit(solution)/shard_map/ppermute | solution.py:48
  (38 other events, 1445.4 us)
Sparse Core Ops, SparseCore 0:
  57.8 59.4 all-gather.1
  576.5 98.1 reduce-scatter.1
